TPU v7x, 32 devices: a whole 2x2x4 slice. The times are simulated.
32 devices in a mesh: groups: 1, rows: 32 (over z, y, x, core).
Axes of the slice: x: 2, y: 2, z: 4, core: 2. Of those that a mesh axis runs over, the one named last changes fastest.
Arguments:
- acts: bfloat16 [4096, 2, 4096], P(('groups', 'rows')), may hold values from -6 to 6
- grads_out: bfloat16 [4096, 2, 4096], P(('groups', 'rows')), may hold values from -6 to 6
- lengths: int32 [32], P('groups'), may hold values from 1 to 512, 4096 in all
- valid: int32 [4096], P(('groups', 'rows')), may hold values 0 or 1
- proj_in: bfloat16 [4096, 128], replicated, may hold values from -0.09375 to 0.09375
- proj_out: bfloat16 [4096, 128], replicated, may hold values from -0.09375 to 0.09375
- fisher_inv: float32 [2, 4096, 4096], P(None, 'rows'), may hold values from -1 to 2, as said below
- database: float32 [4096, 2, 4096], P(('groups', 'rows')), may hold values from -250 to 250
Outputs:
- zscores: float32 [32, 4096], P(None, ('groups', 'rows'))
Inputs may be any that keep to these rules, and one draw needn't show every extreme that they name: The lengths sum to 4096; the largest is exactly 512. `fisher_inv`: each of the 2 blocks is symmetric.
All inputs are finite; a program needn't handle non-finite values. No bound on the sum of `valid` on one device may be relied on, other than what follows from the above.
Results may differ from a plain program's by a relative error of at most 0.0042.
Values sent between devices are 32-bit elements; how exact they have to be, the bound alone decides.
No kernel may reach another device: no remote copies, remote signals or barrier semaphores. Data moves between devices by JAX's collectives and lax.ppermute only.
A program may use at most 64 MiB of HBM per device.

v0:
```python
import jax
import jax.numpy as jnp
from jax import lax
from jax.sharding import PartitionSpec as P


def shards(acts, grads_out, lengths, valid, proj_in, proj_out, fisher_inv, database):
    tok_rows = acts.shape[0]
    modules = acts.shape[1]
    proj_rank = proj_in.shape[1] // modules
    queries = lengths.shape[0]
    flat_width = proj_rank * proj_rank
    first_pos = lax.axis_index("rows") * tok_rows
    positions = first_pos + jnp.arange(tok_rows, dtype=jnp.int32)
    seg_ends = jnp.cumsum(lengths)
    segment = jnp.sum((seg_ends[None, :] <= positions[:, None]).astype(jnp.int32), axis=1)
    selector = (
        (segment[:, None] == jnp.arange(queries, dtype=jnp.int32)[None, :]) & (valid[:, None] == 1)
    ).astype(jnp.bfloat16)
    module_sums = []
    for m in range(modules):
        act_proj = jnp.dot(
            acts[:, m, :],
            proj_in[:, m * proj_rank : (m + 1) * proj_rank],
            preferred_element_type=jnp.float32,
        ).astype(jnp.bfloat16)
        grad_proj = jnp.dot(
            grads_out[:, m, :],
            proj_out[:, m * proj_rank : (m + 1) * proj_rank],
            preferred_element_type=jnp.float32,
        ).astype(jnp.bfloat16)
        spread = (selector[:, :, None] * grad_proj[:, None, :]).reshape(
            tok_rows, queries * proj_rank
        )
        module_sum = lax.dot_general(
            spread, act_proj, (((0,), (0,)), ((), ())), preferred_element_type=jnp.float32
        )
        module_sums.append(module_sum.reshape(queries, flat_width))
    partial_value = jnp.stack(module_sums, axis=1)
    summed = lax.psum(partial_value, "rows")
    precond_cols = jnp.einsum("qmk,mck->qmc", summed, fisher_inv, precision=lax.Precision.HIGHEST)
    scores = jnp.einsum(
        "qmk,nmk->qn",
        lax.all_gather(precond_cols, "rows", axis=2, tiled=True),
        database,
        precision=lax.Precision.HIGHEST,
    )
    db_count = database.shape[0] * lax.axis_size("rows")
    first_moment, second_moment = lax.psum(
        (jnp.sum(scores, axis=1), jnp.sum(scores * scores, axis=1)), "rows"
    )
    avg_score = first_moment / db_count
    variance = second_moment / db_count - avg_score * avg_score
    centred = scores - avg_score[:, None]
    return centred * lax.rsqrt(variance + 1e-06)[:, None]


def solution(mesh):
    placed = (
        P(("groups", "rows"), None, None),
        P(("groups", "rows"), None, None),
        P("groups"),
        P(("groups", "rows")),
        P(),
        P(),
        P(None, "rows", None),
        P(("groups", "rows"), None, None),
    )
    return jax.shard_map(
        shards, mesh=mesh, in_specs=placed, out_specs=P(None, ("groups", "rows")), check_vma=False
    )
```

profile of v0, /device:TPU:0, one launch (start us, length us, event | category | flops | bytes accessed | tf_op | source)
XLA Modules:
  0.0 286.0 jit_solution(3558763104719825832)
XLA Ops:
  6.5 0.0 all-reduce.3.cloned.1.call-start
  6.5 0.0 copy-start.4
  6.5 6.1 %fusion.17 = (bf16[128,1,4096]{2,1,0:T(2,128)(2,1)S(1)}, bf16[128,1,4096]{2,1,0:T(2,128)(2,1)S(1)}) fusion(bf16[128,2,4096]{2,1,0:T(2,128)(2,1)} %param.9), kind=kLoop, calls=%fused_computation.33 | loop fusion | bytes 4194304 | tf_op jit(solution)/shard_map/slice | solution.py:28
  12.7 0.0 copy-done.4
  12.7 0.0 copy-start.3
  12.7 0.0 copy-start.5
  12.7 0.0 copy-start
  12.7 1.6 convolution_convert_fusion.1
  14.4 1.3 convolution_convert_fusion.3
  15.7 0.0 copy-done.3
  15.7 0.1 copy.21
  15.8 0.1 reduce-window.8
  15.8 0.1 reduce
  16.0 0.0 copy-done.5
  16.0 0.0 copy-done
  16.0 0.0 copy-start.2
  16.0 5.8 %fusion.16 = (bf16[128,1,4096]{2,1,0:T(2,128)(2,1)}, bf16[128,1,4096]{2,1,0:T(2,128)(2,1)}) fusion(bf16[128,2,4096]{2,1,0:T(2,128)(2,1)S(1)} %copy-done), kind=kLoop, calls=%fused_computation.32 | loop fusion | bytes 4194304 | tf_op jit(solution)/shard_map/slice | solution.py:23
  21.9 0.1 convert_reduce_fusion
  22.0 1.1 broadcast_multiply_fusion.1
  23.0 0.0 copy-done.2
  23.0 0.0 copy-start.1
  23.0 4.6 %fusion.2 = f32[2048,64]{1,0:T(8,128)} fusion(bf16[128,2048]{0,1:T(8,128)(2,1)} %bitcast.27, bf16[128,1,4096]{2,1,0:T(2,128)(2,1)} %get-tuple-element.9, bf16[4096,128]{1,0:T(8,128)(2,1)S(1)} %copy-done.2), kind=kOutput, calls=%fused_computation.7 | convolution fusion | flops 100671488 | bytes 3145728 | tf_op jit(solution)/shard_map/dot_general | solution.py:35
  27.6 2.4 stack_reshape.6
  30.0 0.0 copy-done.1
  30.0 4.0 %fusion.3 = f32[2048,64]{1,0:T(8,128)} fusion(bf16[128,2048]{0,1:T(8,128)(2,1)} %bitcast.26, bf16[128,1,4096]{2,1,0:T(2,128)(2,1)S(1)} %copy-done.1, bf16[4096,128]{1,0:T(8,128)(2,1)S(1)} %copy-done.2), kind=kOutput, calls=%fused_computation.8 | convolution fusion | flops 100671488 | bytes 3145728 | tf_op jit(solution)/shard_map/dot_general | solution.py:35
  34.0 1.6 stack_reshape.7
  35.6 2.1 pad_maximum_fusion
  37.7 0.0 all-reduce.3.cloned.1.call-update
  37.8 0.2 all-gather.2.cloned.1.call-start
  38.0 133.4 %all-reduce.3.cloned.1.call-done = f32[32,2,4096]{2,0,1:T(8,128)} async-done(((f32[32,2,4096]{2,0,1:T(8,128)}), f32[32,2,4096]{2,0,1:T(8,128)}) %all-reduce.3.cloned.1.call-update) | async-done | bytes 1048592 | tf_op jit(solution)/shard_map/psum | solution.py:40
  171.4 7.3 %convolution_bitcast_fusion = f32[32,2,128]{2,0,1:T(8,128)} fusion(f32[32,2,4096]{2,0,1:T(8,128)} %all-reduce.3.cloned.1.call-done, f32[2,128,4096]{2,1,0:T(8,128)} %param.14), kind=kOutput, calls=%fused_computation.2 | convolution fusion | flops 402653184 | bytes 5275648 | tf_op jit(solution)/shard_map/qmk,mck->qmc/dot_general | solution.py:41
  178.7 0.0 all-gather.2.cloned.1.call-update
  178.8 51.4 %all-gather.2.cloned.1.call-done = f32[32,2,4096]{2,0,1:T(8,128)} async-done(((f32[32,2,128]{2,0,1:T(8,128)}), f32[32,2,4096]{2,0,1:T(8,128)}) %all-gather.2.cloned.1.call-update) | async-done | bytes 1048592 | tf_op jit(solution)/shard_map/all_gather | solution.py:44
  230.2 8.2 %fusion.15 = (f32[32]{0:T(128)S(1)}, f32[32]{0:T(128)S(1)}, f32[32,128]{1,0:T(8,128)S(1)}) fusion(f32[32,2,4096]{2,0,1:T(8,128)} %all-gather.2.cloned.1.call-done, f32[128,2,4096]{2,1,0:T(2,128)} %param.15), kind=kOutput, calls=%fused_computation.31 | convolution fusion | flops 402665408 | bytes 5259520 | tf_op jit(solution)/shard_map/qmk,nmk->qn/dot_general | solution.py:42
  238.3 40.1 %all-reduce = (f32[32]{0:T(128)S(1)}, f32[32]{0:T(128)S(1)}) all-reduce(f32[32]{0:T(128)S(1)} %get-tuple-element.6, f32[32]{0:T(128)S(1)} %get-tuple-element.5), channel_id=1, replica_groups=mesh['groups'=1,'rows'=32] {'rows'}, use_global_device_ids=true, to_apply=%region_6.7 | all-reduce | flops 64 | bytes 512 | tf_op jit(solution)/shard_map/psum | solution.py:49
  278.5 0.7 subtract_multiply_fusion
  (4 shorter events, 0.0 us)
Async XLA Ops:
  6.5 164.9 %all-reduce.3.cloned.1.call-start = ((), (), s32[]{:S(2)}) async-start(), calls=%async_computation | async-start | bytes 2097152 | tf_op jit(solution)/shard_map/psum | solution.py:40
  6.5 6.1 %copy-start.4 = (bf16[4096,128]{1,0:T(8,128)(2,1)S(1)}, bf16[4096,128]{1,0:T(8,128)(2,1)}, u32[]{:S(2)}) copy-start(bf16[4096,128]{1,0:T(8,128)(2,1)} %param.13) | copy-start | bytes 3145732
  12.7 3.0 %copy-start.3 = (s32[32]{0:T(128)S(1)}, s32[32]{0:T(128)}, u32[]{:S(2)}) copy-start(s32[32]{0:T(128)} %param.10) | copy-start | bytes 388
  12.7 3.3 %copy-start.5 = (s32[128]{0:T(128)S(1)}, s32[128]{0:T(128)}, u32[]{:S(2)}) copy-start(s32[128]{0:T(128)} %param.11) | copy-start | bytes 1540
  12.7 3.3 %copy-start = (bf16[128,2,4096]{2,1,0:T(2,128)(2,1)S(1)}, bf16[128,2,4096]{2,1,0:T(2,128)(2,1)}, u32[]{:S(2)}) copy-start(bf16[128,2,4096]{2,1,0:T(2,128)(2,1)} %param.8) | copy-start | bytes 6291460
  16.0 7.0 %copy-start.2 = (bf16[4096,128]{1,0:T(8,128)(2,1)S(1)}, bf16[4096,128]{1,0:T(8,128)(2,1)}, u32[]{:S(2)}) copy-start(bf16[4096,128]{1,0:T(8,128)(2,1)} %param.12) | copy-start | bytes 3145732
  23.0 7.0 %copy-start.1 = (bf16[128,1,4096]{2,1,0:T(2,128)(2,1)S(1)}, bf16[128,1,4096]{2,1,0:T(2,128)(2,1)}, u32[]{:S(2)}) copy-start(bf16[128,1,4096]{2,1,0:T(2,128)(2,1)} %get-tuple-element.10) | copy-start | bytes 3145732
  37.8 192.4 %all-gather.2.cloned.1.call-start = ((), (), s32[]{:S(2)}) async-start(), calls=%async_computation.1 | async-start | bytes 1081344 | tf_op jit(solution)/shard_map/all_gather | solution.py:44
Sparse Core Ops, SparseCore 0:
  37.9 133.4 all-reduce.2
  178.9 51.2 all-gather.1
where the time goes:
time: 286 us
  waiting for transfers between devices  185 us (65%)
  blocking collectives  40.1 us (14%)
  matrix products  27.1 us (9%)
  local copies, waits for them, and re-layouts  16 us (6%)
  between operations  13.5 us (5%)
  other arithmetic  4.19 us (1%)
    psum x1, waiting for transfers between devices, shards(): summed = lax.psum(partial_value, 'rows')  133 us
    all_gather x1, waiting for transfers between devices, shards(): lax.all_gather(precond_cols, 'rows', axis=2, tiled=True)  51.4 us
    psum x1, blocking collectives, shards(): lax.psum((jnp.sum(scores, axis=1), jnp.sum(scores * scores, axis=1)), 'ro...  40.1 us
    dot_general x2, matrix products, shards(): lax.dot_general(spread, act_proj, (((0,), (0,)), ((), ())), preferred_ele...  8.6 us
    dot_general x1, matrix products, shards(): jnp.einsum('qmk,nmk->qn', lax.all_gather(precond_cols, 'rows', axis=2, ti...  8.16 us
    dot_general x1, matrix products, shards(): jnp.einsum('qmk,mck->qmc', summed, fisher_inv, precision=lax.Precision.HI...  7.35 us
    slice x1, local copies, waits for them, and re-layouts, shards(): grads_out[:, m, :]  6.11 us
    slice x1, local copies, waits for them, and re-layouts, shards(): acts[:, m, :]  5.84 us
  transfers between devices with their start and end apart: 2, of which 2 were waited for; matrix products, arithmetic and copies ran while one was open for 0% of the time, Pallas kernels for 0%

commit v1 on v0

--- a/solution.py
+++ b/solution.py
@@ -37,7 +37,9 @@
         )
         module_sums.append(module_sum.reshape(queries, flat_width))
     partial_value = jnp.stack(module_sums, axis=1)
-    summed = lax.psum(partial_value, "rows")
+    summed = partial_value
+    for hop in (1, 2, 4, 8, 16):
+        summed = summed + lax.ppermute(summed, "rows", [(dev, dev ^ hop) for dev in range(32)])
     precond_cols = jnp.einsum("qmk,mck->qmc", summed, fisher_inv, precision=lax.Precision.HIGHEST)
     scores = jnp.einsum(
         "qmk,nmk->qn",

time: 286 us -> 278 us (0.972)
  waiting for transfers between devices: 185 us -> 168 us
  starting transfers between devices: 0.22 us -> 9.19 us
  matrix products: 27.1 us -> 24 us
  local copies, waits for them, and re-layouts: 16 us -> 19 us
    psum x1 -> x0, waiting for transfers between devices: 133 us -> none  [shards(): summed = lax.psum(partial_value, 'rows')]
    ppermute x0 -> x5, waiting for transfers between devices: none -> 115 us  [shards(): lax.ppermute(summed, 'rows', [(dev, dev ^ hop) for dev in range(32)])]
    ppermute x0 -> x5, starting transfers between devices: none -> 9.19 us  [shards(): lax.ppermute(summed, 'rows', [(dev, dev ^ hop) for dev in range(32)])]
  transfers between devices with their start and end apart: 2 -> 6, of which waited for: 2 -> 6; matrix products, arithmetic and copies ran while one was open for 0% -> 0% of each run, Pallas kernels for 0% -> 0%
where the time goes in v1:
time: 278 us; the launch traced here: 277 us
  waiting for transfers between devices  168 us (60%)
  blocking collectives  40.1 us (14%)
  matrix products  24 us (9%)
  local copies, waits for them, and re-layouts  19 us (7%)
  between operations  13.5 us (5%)
  starting transfers between devices  9.19 us (3%)
  other arithmetic  3.53 us (1%)
    ppermute x5, waiting for transfers between devices, shards(): lax.ppermute(summed, 'rows', [(dev, dev ^ hop) for dev in range(32)])  115 us
    all_gather x1, waiting for transfers between devices, shards(): lax.all_gather(precond_cols, 'rows', axis=2, tiled=True)  53 us
    psum x1, blocking collectives, shards(): lax.psum((jnp.sum(scores, axis=1), jnp.sum(scores * scores, axis=1)), 'ro...  40.1 us
    ppermute x5, starting transfers between devices, shards(): lax.ppermute(summed, 'rows', [(dev, dev ^ hop) for dev in range(32)])  9.19 us
    dot_general x2, matrix products, shards(): lax.dot_general(spread, act_proj, (((0,), (0,)), ((), ())), preferred_ele...  8.27 us
    dot_general x1, matrix products, shards(): jnp.einsum('qmk,nmk->qn', lax.all_gather(precond_cols, 'rows', axis=2, ti...  8.16 us
    slice x1, local copies, waits for them, and re-layouts, shards(): grads_out[:, m, :]  6.27 us
    slice x1, local copies, waits for them, and re-layouts, shards(): acts[:, m, :]  5.82 us
  transfers between devices with their start and end apart: 6, of which 6 were waited for; matrix products, arithmetic and copies ran while one was open for 0% of the time, Pallas kernels for 0%

profile of v1, /device:TPU:0, one launch (start us, length us, event | category | flops | bytes accessed | tf_op | source)
XLA Modules:
  0.0 277.5 jit_solution(10707932408609208104)
XLA Ops:
  6.5 0.0 all-gather.2.cloned.1.call-start
  6.5 0.0 copy-start.5
  6.5 6.3 %fusion.18 = (bf16[128,1,4096]{2,1,0:T(2,128)(2,1)S(1)}, bf16[128,1,4096]{2,1,0:T(2,128)(2,1)S(1)}) fusion(bf16[128,2,4096]{2,1,0:T(2,128)(2,1)} %param.9), kind=kLoop, calls=%fused_computation.35 | loop fusion | bytes 4194304 | tf_op jit(solution)/shard_map/slice | solution.py:28
  12.8 0.0 copy-done.5
  12.8 0.0 copy-start.4
  12.8 0.0 copy-start.6
  12.9 0.0 copy-start
  12.9 1.6 convolution_convert_fusion.1
  14.5 1.3 convolution_convert_fusion.3
  15.9 0.0 copy-done.4
  15.9 0.1 copy.21
  16.0 0.1 reduce-window.8
  16.0 0.1 reduce
  16.1 0.0 copy-done.6
  16.2 0.0 copy-done
  16.2 0.0 copy-start.2
  16.2 5.8 %fusion.17 = (bf16[128,1,4096]{2,1,0:T(2,128)(2,1)}, bf16[128,1,4096]{2,1,0:T(2,128)(2,1)}) fusion(bf16[128,2,4096]{2,1,0:T(2,128)(2,1)S(1)} %copy-done), kind=kLoop, calls=%fused_computation.34 | loop fusion | bytes 4194304 | tf_op jit(solution)/shard_map/slice | solution.py:23
  22.0 0.1 convert_reduce_fusion
  22.1 0.9 broadcast_multiply_fusion
  23.0 0.0 copy-done.2
  23.0 4.3 %fusion.2 = f32[2048,64]{1,0:T(8,128)} fusion(bf16[128,2048]{0,1:T(8,128)(2,1)S(1)} %bitcast.26, bf16[128,1,4096]{2,1,0:T(2,128)(2,1)} %get-tuple-element.10, bf16[4096,128]{1,0:T(8,128)(2,1)S(1)} %copy-done.2), kind=kOutput, calls=%fused_computation.7 | convolution fusion | flops 100671488 | bytes 3145728 | tf_op jit(solution)/shard_map/dot_general | solution.py:35
  27.3 0.0 copy-start.1
  27.3 2.5 stack_reshape.6
  29.8 1.9 constant_dynamic-update-slice_fusion.1
  31.7 0.0 copy-done.1
  31.7 4.0 %fusion.3 = f32[2048,64]{1,0:T(8,128)} fusion(bf16[128,2048]{0,1:T(8,128)(2,1)} %bitcast.25, bf16[128,1,4096]{2,1,0:T(2,128)(2,1)S(1)} %copy-done.1, bf16[4096,128]{1,0:T(8,128)(2,1)S(1)} %copy-done.2), kind=kOutput, calls=%fused_computation.8 | convolution fusion | flops 100671488 | bytes 3145728 | tf_op jit(solution)/shard_map/dot_general | solution.py:35
  35.7 1.6 stack_reshape.7
  37.2 0.8 constant_dynamic-update-slice_fusion
  38.1 0.5 collective-permute-start
  38.6 2.5 collective-permute-done
  41.1 1.3 add.37
  42.4 2.9 %collective-permute-start.1 = (f32[32,2,4096]{2,0,1:T(8,128)S(1)}, f32[32,2,4096]{2,0,1:T(8,128)S(1)}, u32[]{:S(2)}, u32[]{:S(2)}) collective-permute-start(f32[32,2,4096]{2,0,1:T(8,128)S(1)} %add.37), channel_id=1, source_target_pairs={{0,2},{1,3},{2,0},{3,1},{4,6},{5,7},{6,4},{7,5},{8,10},{9,11},{10,... | collective-permute-start | bytes 3145736 | tf_op jit(solution)/shard_map/ppermute | solution.py:42
  45.3 23.5 %collective-permute-done.1 = f32[32,2,4096]{2,0,1:T(8,128)S(1)} collective-permute-done((f32[32,2,4096]{2,0,1:T(8,128)S(1)}, f32[32,2,4096]{2,0,1:T(8,128)S(1)}, u32[]{:S(2)}, u32[]{:S(2)}) %collective-permute-start.1) | collective-permute-done | bytes 1048608 | tf_op jit(solution)/shard_map/ppermute | solution.py:42
  68.8 0.1 add.38
  68.9 1.8 collective-permute-start.2
  70.7 22.9 %collective-permute-done.2 = f32[32,2,4096]{2,0,1:T(8,128)S(1)} collective-permute-done((f32[32,2,4096]{2,0,1:T(8,128)S(1)}, f32[32,2,4096]{2,0,1:T(8,128)S(1)}, u32[]{:S(2)}, u32[]{:S(2)}) %collective-permute-start.2) | collective-permute-done | bytes 1048608 | tf_op jit(solution)/shard_map/ppermute | solution.py:42
  93.6 0.0 copy-start.3
  93.6 0.1 add.39
  93.7 1.6 collective-permute-start.3
  95.3 22.2 %collective-permute-done.3 = f32[32,2,4096]{2,0,1:T(8,128)S(1)} collective-permute-done((f32[32,2,4096]{2,0,1:T(8,128)S(1)}, f32[32,2,4096]{2,0,1:T(8,128)S(1)}, u32[]{:S(2)}, u32[]{:S(2)}) %collective-permute-start.3) | collective-permute-done | bytes 1048608 | tf_op jit(solution)/shard_map/ppermute | solution.py:42
  117.5 0.1 add.40
  117.7 2.3 collective-permute-start.4
  120.0 44.0 %collective-permute-done.4 = f32[32,2,4096]{2,0,1:T(8,128)S(1)} collective-permute-done((f32[32,2,4096]{2,0,1:T(8,128)S(1)}, f32[32,2,4096]{2,0,1:T(8,128)S(1)}, u32[]{:S(2)}, u32[]{:S(2)}) %collective-permute-start.4) | collective-permute-done | bytes 1048608 | tf_op jit(solution)/shard_map/ppermute | solution.py:42
  164.0 0.0 copy-done.3
  164.0 4.6 %convolution_bitcast_fusion = f32[32,2,128]{2,0,1:T(8,128)} fusion(f32[2,128,4096]{2,1,0:T(8,128)S(1)} %copy-done.3, f32[32,2,4096]{2,0,1:T(8,128)S(1)} %add.40, f32[32,2,4096]{2,0,1:T(8,128)S(1)} %collective-permute-done.4), kind=kOutput, calls=%fused_computation.2 | convolution fusion | flops 402915328 | bytes 6324224 | tf_op jit(solution)/shard_map/qmk,mck->qmc/dot_general | solution.py:43
  168.6 0.0 all-gather.2.cloned.1.call-update
  168.6 53.0 %all-gather.2.cloned.1.call-done = f32[32,2,4096]{2,0,1:T(8,128)} async-done(((f32[32,2,128]{2,0,1:T(8,128)}), f32[32,2,4096]{2,0,1:T(8,128)}) %all-gather.2.cloned.1.call-update) | async-done | bytes 1048592 | tf_op jit(solution)/shard_map/all_gather | solution.py:46
  221.6 8.2 %fusion.16 = (f32[32]{0:T(128)S(1)}, f32[32]{0:T(128)S(1)}, f32[32,128]{1,0:T(8,128)S(1)}) fusion(f32[32,2,4096]{2,0,1:T(8,128)} %all-gather.2.cloned.1.call-done, f32[128,2,4096]{2,1,0:T(2,128)} %param.15), kind=kOutput, calls=%fused_computation.33 | convolution fusion | flops 402665408 | bytes 5259520 | tf_op jit(solution)/shard_map/qmk,nmk->qn/dot_general | solution.py:44
  229.8 40.1 %all-reduce = (f32[32]{0:T(128)S(1)}, f32[32]{0:T(128)S(1)}) all-reduce(f32[32]{0:T(128)S(1)} %get-tuple-element.6, f32[32]{0:T(128)S(1)} %get-tuple-element.5), channel_id=1, replica_groups=mesh['groups'=1,'rows'=32] {'rows'}, use_global_device_ids=true, to_apply=%region_5.6 | all-reduce | flops 64 | bytes 512 | tf_op jit(solution)/shard_map/psum | solution.py:51
  269.9 0.7 subtract_multiply_fusion
  (4 shorter events, 0.0 us)
Async XLA Ops:
  6.5 215.1 %all-gather.2.cloned.1.call-start = ((), (), s32[]{:S(2)}) async-start(), calls=%async_computation | async-start | bytes 1081344 | tf_op jit(solution)/shard_map/all_gather | solution.py:46
  6.5 6.3 %copy-start.5 = (bf16[4096,128]{1,0:T(8,128)(2,1)S(1)}, bf16[4096,128]{1,0:T(8,128)(2,1)}, u32[]{:S(2)}) copy-start(bf16[4096,128]{1,0:T(8,128)(2,1)} %param.13) | copy-start | bytes 3145732
  12.8 3.0 %copy-start.4 = (s32[32]{0:T(128)S(1)}, s32[32]{0:T(128)}, u32[]{:S(2)}) copy-start(s32[32]{0:T(128)} %param.10) | copy-start | bytes 388
  12.8 3.3 %copy-start.6 = (s32[128]{0:T(128)S(1)}, s32[128]{0:T(128)}, u32[]{:S(2)}) copy-start(s32[128]{0:T(128)} %param.11) | copy-start | bytes 1540
  12.9 3.3 %copy-start = (bf16[128,2,4096]{2,1,0:T(2,128)(2,1)S(1)}, bf16[128,2,4096]{2,1,0:T(2,128)(2,1)}, u32[]{:S(2)}) copy-start(bf16[128,2,4096]{2,1,0:T(2,128)(2,1)} %param.8) | copy-start | bytes 6291460
  16.2 6.8 %copy-start.2 = (bf16[4096,128]{1,0:T(8,128)(2,1)S(1)}, bf16[4096,128]{1,0:T(8,128)(2,1)}, u32[]{:S(2)}) copy-start(bf16[4096,128]{1,0:T(8,128)(2,1)} %param.12) | copy-start | bytes 3145732
  27.3 4.4 %copy-start.1 = (bf16[128,1,4096]{2,1,0:T(2,128)(2,1)S(1)}, bf16[128,1,4096]{2,1,0:T(2,128)(2,1)}, u32[]{:S(2)}) copy-start(bf16[128,1,4096]{2,1,0:T(2,128)(2,1)} %get-tuple-element.9) | copy-start | bytes 3145732
  38.1 3.0 %collective-permute-start = (f32[32,2,4096]{2,0,1:T(8,128)}, f32[32,2,4096]{2,0,1:T(8,128)S(1)}, u32[]{:S(2)}, u32[]{:S(2)}) collective-permute-start(f32[32,2,4096]{2,0,1:T(8,128)} %constant_dynamic-update-slice_fusion), channel_id=1, source_target_pairs={{0,1},{1,0},{2,3},{3,2},{4,5},{5,4},{6,7},{7,6},{8,9},{9,8},{10,11... | collective-permute-start | bytes 3145736 | tf_op jit(solution)/shard_map/ppermute | solution.py:42
  42.4 26.4 %collective-permute-start.1 = (f32[32,2,4096]{2,0,1:T(8,128)S(1)}, f32[32,2,4096]{2,0,1:T(8,128)S(1)}, u32[]{:S(2)}, u32[]{:S(2)}) collective-permute-start(f32[32,2,4096]{2,0,1:T(8,128)S(1)} %add.37), channel_id=1, source_target_pairs={{0,2},{1,3},{2,0},{3,1},{4,6},{5,7},{6,4},{7,5},{8,10},{9,11},{10,... | collective-permute-start | bytes 3145736 | tf_op jit(solution)/shard_map/ppermute | solution.py:42
  68.9 24.7 %collective-permute-start.2 = (f32[32,2,4096]{2,0,1:T(8,128)S(1)}, f32[32,2,4096]{2,0,1:T(8,128)S(1)}, u32[]{:S(2)}, u32[]{:S(2)}) collective-permute-start(f32[32,2,4096]{2,0,1:T(8,128)S(1)} %add.38), channel_id=1, source_target_pairs={{0,4},{1,5},{2,6},{3,7},{4,0},{5,1},{6,2},{7,3},{8,12},{9,13},{10,... | collective-permute-start | bytes 3145736 | tf_op jit(solution)/shard_map/ppermute | solution.py:42
  93.6 70.4 %copy-start.3 = (f32[2,128,4096]{2,1,0:T(8,128)S(1)}, f32[2,128,4096]{2,1,0:T(8,128)}, u32[]{:S(2)}) copy-start(f32[2,128,4096]{2,1,0:T(8,128)} %param.14) | copy-start | bytes 12582916
  93.7 23.8 %collective-permute-start.3 = (f32[32,2,4096]{2,0,1:T(8,128)S(1)}, f32[32,2,4096]{2,0,1:T(8,128)S(1)}, u32[]{:S(2)}, u32[]{:S(2)}) collective-permute-start(f32[32,2,4096]{2,0,1:T(8,128)S(1)} %add.39), channel_id=1, source_target_pairs={{0,8},{1,9},{2,10},{3,11},{4,12},{5,13},{6,14},{7,15},{8,0},{9,1},... | collective-permute-start | bytes 3145736 | tf_op jit(solution)/shard_map/ppermute | solution.py:42
  117.7 46.3 %collective-permute-start.4 = (f32[32,2,4096]{2,0,1:T(8,128)S(1)}, f32[32,2,4096]{2,0,1:T(8,128)S(1)}, u32[]{:S(2)}, u32[]{:S(2)}) collective-permute-start(f32[32,2,4096]{2,0,1:T(8,128)S(1)} %add.40), channel_id=1, source_target_pairs={{0,16},{1,17},{2,18},{3,19},{4,20},{5,21},{6,22},{7,23},{8,24},{9,... | collective-permute-start | bytes 3145736 | tf_op jit(solution)/shard_map/ppermute | solution.py:42
Sparse Core Ops, SparseCore 0:
  168.8 52.8 all-gather.1
